TPU v7x, 32 devices: a whole 2x2x4 slice. The times are simulated.
32 devices in a mesh: user: 8 (over z, y), item: 4 (over x, core).
Axes of the slice: x: 2, y: 2, z: 4, core: 2. Of those that a mesh axis runs over, the one named last changes fastest.
Arguments:
- theta_shape: float32 [16384, 1024], P('user', 'item'), may hold values from 0.3 to 3
- theta_rate: float32 [16384, 1024], P('user', 'item'), may hold values from 100 to 1000
- xi_rate: float32 [16384], P('user'), may hold values from 1 to 10
- beta_shape: float32 [4096, 1024], P('item', 'user'), may hold values from 0.3 to 3
- beta_rate: float32 [4096, 1024], P('item', 'user'), may hold values from 50 to 500
- eta_rate: float32 [4096], P('item'), may hold values from 1 to 10
- tile_slots: int32 [8, 4, 32], P('user', 'item'), may hold values from 0 to 31, as said below
- tile_counts: bfloat16 [8, 4, 32, 256, 256], P('user', 'item'), may hold values from 0 to 5, as said below
- live_tiles: int32 [8, 4], P('user', 'item'), may hold values from 1 to 32, as said below
Outputs:
- theta_shape_new: float32 [16384, 1024], P('user', 'item')
- theta_log_rate: float32 [16384, 1024], P('user', 'item')
- xi_rate_new: float32 [16384], P('user')
- beta_shape_new: float32 [4096, 1024], P('item', 'user')
- beta_log_rate: float32 [4096, 1024], P('item', 'user')
- eta_rate_new: float32 [4096], P('item')
Inputs may be any that keep to these rules, and one draw needn't show every extreme that they name: `tile_slots`: within one device's 32 slots the positions are distinct. `tile_counts`: whole numbers. `live_tiles`: some device uses all 32 slots.
All inputs are finite; a program needn't handle non-finite values.
Results may differ from a plain program's by a relative error of at most 0.0029.
Values may be sent and summed in bfloat16 or wider, within the bound.
No kernel may reach another device: no remote copies, remote signals or barrier semaphores. Data moves between devices by JAX's collectives and lax.ppermute only.
A program may use at most 128 MiB of HBM per device.

v0:
```python
import math
import jax
import jax.numpy as jnp
from jax import lax
from jax.sharding import PartitionSpec as P

BLK = 256
UB = 8
IB = 4
TMAX = 32
prior_a = 0.3
prior_a2 = 0.3
prior_b2 = 1.0
prior_c = 0.3
prior_c2 = 0.3
prior_d2 = 1.0


def exp_mean_log(shape_param, rate_param):
    return jnp.exp(lax.digamma(shape_param) - jnp.log(rate_param)).astype(jnp.bfloat16)


def on_device(
    theta_shape,
    theta_rate,
    xi_rate,
    beta_shape,
    beta_rate,
    eta_rate,
    tile_slots,
    tile_counts,
    live_tiles,
):
    user_width = lax.axis_size("user")
    item_width = lax.axis_size("item")
    user_index = lax.axis_index("user")
    item_index = lax.axis_index("item")
    theta_part = exp_mean_log(theta_shape, theta_rate)
    beta_part = exp_mean_log(beta_shape, beta_rate)
    theta_full = lax.all_gather(theta_part, "item", axis=1, tiled=True)
    beta_full = lax.all_gather(beta_part, "user", axis=1, tiled=True)
    factors = theta_full.shape[1]
    user_rows = theta_full.shape[0]
    item_rows = beta_full.shape[0]
    theta_blocks = theta_full.reshape(UB, BLK, factors)
    beta_blocks = beta_full.reshape(IB, BLK, factors)
    slot_list = tile_slots.reshape(TMAX)
    count_tiles = tile_counts.reshape(TMAX, BLK, BLK)
    used_slots = live_tiles.reshape(())
    user_blocks = slot_list // IB
    item_blocks = slot_list % IB
    group_size = math.gcd(TMAX, 8)

    def group_step(group_index, carried):
        user_acc, item_acc = carried
        first_slot = group_index * group_size
        rows_user = lax.dynamic_slice_in_dim(user_blocks, first_slot, group_size, 0)
        rows_item = lax.dynamic_slice_in_dim(item_blocks, first_slot, group_size, 0)
        counts = lax.dynamic_slice_in_dim(count_tiles, first_slot, group_size, 0).astype(
            jnp.float32
        )
        slot_mask = (first_slot + jnp.arange(group_size) < used_slots).astype(jnp.float32)
        counts = counts * slot_mask[:, None, None]
        users = jnp.take(theta_blocks, rows_user, axis=0)
        items = jnp.take(beta_blocks, rows_item, axis=0)
        denominator = jnp.einsum("tuk,tik->tui", users, items, preferred_element_type=jnp.float32)
        ratio_tile = (counts / denominator).astype(jnp.bfloat16)
        user_terms = jnp.einsum(
            "tui,tik->tuk", ratio_tile, items, preferred_element_type=jnp.float32
        )
        item_terms = jnp.einsum(
            "tui,tuk->tik", ratio_tile, users, preferred_element_type=jnp.float32
        )
        user_acc = user_acc.at[rows_user].add(user_terms)
        item_acc = item_acc.at[rows_item].add(item_terms)
        return (user_acc, item_acc)

    start_acc = (
        jnp.zeros((UB, BLK, factors), jnp.float32),
        jnp.zeros((IB, BLK, factors), jnp.float32),
    )
    group_count = TMAX // group_size
    user_acc, item_acc = lax.fori_loop(0, group_count, group_step, start_acc)
    user_acc = user_acc.reshape(user_rows, factors)
    item_acc = item_acc.reshape(item_rows, factors)
    beta_columns = factors // user_width
    theta_columns = factors // item_width
    beta_local = jnp.sum(beta_shape / beta_rate, axis=0)
    theta_local = jnp.sum(theta_shape / theta_rate, axis=0)
    beta_placed = lax.dynamic_update_slice_in_dim(
        jnp.zeros((factors,), jnp.float32), beta_local, user_index * beta_columns, 0
    )
    theta_placed = lax.dynamic_update_slice_in_dim(
        jnp.zeros((factors,), jnp.float32), theta_local, item_index * theta_columns, 0
    )
    beta_total, theta_total = lax.psum((beta_placed, theta_placed), ("user", "item"))
    xi_mean = (prior_a2 + factors * prior_a) / xi_rate
    user_summed = lax.psum(user_acc, "item")
    shape_whole = prior_a + theta_full.astype(jnp.float32) * user_summed
    rate_whole = xi_mean[:, None] + beta_total[None, :]
    xi_rate_new = prior_a2 / prior_b2 + jnp.sum(shape_whole / rate_whole, axis=1)
    theta_shape_new = lax.dynamic_slice_in_dim(
        shape_whole, item_index * theta_columns, theta_columns, 1
    )
    theta_rate_new = lax.dynamic_slice_in_dim(
        rate_whole, item_index * theta_columns, theta_columns, 1
    )
    item_share = lax.psum_scatter(item_acc, "user", scatter_dimension=1, tiled=True)
    beta_shape_new = prior_c + beta_part.astype(jnp.float32) * item_share
    eta_mean = (prior_c2 + factors * prior_c) / eta_rate
    theta_slice = lax.dynamic_slice_in_dim(theta_total, user_index * beta_columns, beta_columns, 0)
    beta_rate_new = eta_mean[:, None] + theta_slice[None, :]
    item_part = jnp.sum(beta_shape_new / beta_rate_new, axis=1)
    eta_rate_new = prior_c2 / prior_d2 + lax.psum(item_part, "user")
    return (
        theta_shape_new,
        jnp.log(theta_rate_new),
        xi_rate_new,
        beta_shape_new,
        jnp.log(beta_rate_new),
        eta_rate_new,
    )


def solution(mesh):
    in_specs = (
        P("user", "item"),
        P("user", "item"),
        P("user"),
        P("item", "user"),
        P("item", "user"),
        P("item"),
        P("user", "item", None),
        P("user", "item", None, None, None),
        P("user", "item"),
    )
    out_specs = (
        P("user", "item"),
        P("user", "item"),
        P("user"),
        P("item", "user"),
        P("item", "user"),
        P("item"),
    )
    return jax.shard_map(
        on_device, mesh=mesh, in_specs=in_specs, out_specs=out_specs, check_vma=False
    )
```

profile of v0, /device:TPU:0, one launch (start us, length us, event | category | flops | bytes accessed | tf_op | source)
XLA Modules:
  0.0 632.4 jit_solution(3128361467981943288)
XLA Ops:
  7.2 6.0 fusion.22
  13.3 17.6 %fusion.16 = (bf16[2048,256]{1,0:T(8,128)(2,1)}, f32[256]{0:T(256)}) fusion(f32[2048,256]{1,0:T(8,128)} %param.12, f32[2048,256]{1,0:T(8,128)} %param.11), kind=kLoop, calls=%fused_computation.36 | loop fusion | flops 41418496 | bytes 5243904 | tf_op jit(solution)/shard_map/convert_element_type | solution.py:20
  30.9 35.5 %all-gather.5.cloned.1.call-done = bf16[1024,1024]{1,0:T(8,128)(2,1)} async-done(((bf16[1024,128]{1,0:T(8,128)(2,1)}), bf16[1024,1024]{1,0:T(8,128)(2,1)}) %all-gather.5.cloned.1.call-update) | async-done | bytes 2097168 | tf_op jit(solution)/shard_map/all_gather | solution.py:41
  66.4 35.3 %all-gather.3.cloned.1.call-done = bf16[2048,1024]{1,0:T(8,128)(2,1)} async-done(((bf16[2048,256]{1,0:T(8,128)(2,1)}), bf16[2048,1024]{1,0:T(8,128)(2,1)}) %all-gather.3.cloned.1.call-update) | async-done | bytes 4194320 | tf_op jit(solution)/shard_map/all_gather | solution.py:40
  108.5 246.7 %while.15 = (s32[]{:T(128)}, f32[8,256,1024]{2,1,0:T(8,128)}, f32[4,256,1024]{2,1,0:T(8,128)}, s32[32]{0:T(128)S(1)}, bf16[32,256,256]{2,1,0:T(8,128)(2,1)}, /*i...) while((s32[]{:T(128)}, f32[8,256,1024]{2,1,0:T(8,128)}, ...), condition=%wide.region_3.4_spmd, body=%wide.region_0.3_spmd.sunk | while | flops 3238004736 | bytes 134226640 | solution.py:83
  108.6 5.0 gather_fusion
  116.4 5.0 fusion.28
  122.1 6.0 fusion.30
  128.1 17.1 %scatter_fusion.1 = f32[4,256,1024]{2,1,0:T(8,128)} fusion(f32[4,256,1024]{2,1,0:T(8,128)} %get-tuple-element.281, s32[8]{0:T(128)S(1)} %get-tuple-element.264, f32[8,256,1024]{2,1,0:T(8,128)} %fusion.30), kind=kCustom, calls=%fused_computation.3.clone.1 | custom fusion | flops 2097152 | bytes 25165856 | tf_op jit(solution)/shard_map/while/body/eval_jaxpr/scatter-add | solution.py:75
  145.2 7.7 %fusion.29 = f32[8,256,1024]{2,1,0:T(8,128)} fusion(f32[8,256,256]{2,1,0:T(8,128)} %copy-done.8, bf16[8,256,1024]{2,1,0:T(8,128)(2,1)} %gather_fusion.1, pred[8]{0:T(512)(128)(4,1)S(1)} %get-tuple-element.265, f32[8]{0:T(128)S(1)} %compare_convert_fusion.2, bf16[32,256,256]{2,1,0:T(8,128)(2,1)} %get-tuple-element.296, s32[]{:T(128)S(6)} %select_n.90), kind=kOutput, calls=%fused_computation.8.clone.1 | convolution fusion | flops 1077936128 | bytes 15728684 | tf_op jit(solution)/shard_map/while/body/eval_jaxpr/tui,tik->tuk/dot_general | solution.py:68
  152.9 17.4 %scatter_fusion = f32[8,256,1024]{2,1,0:T(8,128)} fusion(f32[8,256,1024]{2,1,0:T(8,128)} %get-tuple-element.280, s32[8]{0:T(128)S(1)} %get-tuple-element.262, f32[8,256,1024]{2,1,0:T(8,128)} %fusion.29), kind=kCustom, calls=%fused_computation.2.clone.1 | custom fusion | flops 2097152 | bytes 25165856 | tf_op jit(solution)/shard_map/while/body/eval_jaxpr/scatter-add | solution.py:74
  170.4 5.0 gather_fusion
  178.2 5.0 fusion.28
  183.9 6.0 fusion.30
  189.9 17.1 %scatter_fusion.1 = f32[4,256,1024]{2,1,0:T(8,128)} fusion(f32[4,256,1024]{2,1,0:T(8,128)} %get-tuple-element.281, s32[8]{0:T(128)S(1)} %get-tuple-element.264, f32[8,256,1024]{2,1,0:T(8,128)} %fusion.30), kind=kCustom, calls=%fused_computation.3.clone.1 | custom fusion | flops 2097152 | bytes 25165856 | tf_op jit(solution)/shard_map/while/body/eval_jaxpr/scatter-add | solution.py:75
  207.0 7.7 %fusion.29 = f32[8,256,1024]{2,1,0:T(8,128)} fusion(f32[8,256,256]{2,1,0:T(8,128)} %copy-done.8, bf16[8,256,1024]{2,1,0:T(8,128)(2,1)} %gather_fusion.1, pred[8]{0:T(512)(128)(4,1)S(1)} %get-tuple-element.265, f32[8]{0:T(128)S(1)} %compare_convert_fusion.2, bf16[32,256,256]{2,1,0:T(8,128)(2,1)} %get-tuple-element.296, s32[]{:T(128)S(6)} %select_n.90), kind=kOutput, calls=%fused_computation.8.clone.1 | convolution fusion | flops 1077936128 | bytes 15728684 | tf_op jit(solution)/shard_map/while/body/eval_jaxpr/tui,tik->tuk/dot_general | solution.py:68
  214.7 17.5 %scatter_fusion = f32[8,256,1024]{2,1,0:T(8,128)} fusion(f32[8,256,1024]{2,1,0:T(8,128)} %get-tuple-element.280, s32[8]{0:T(128)S(1)} %get-tuple-element.262, f32[8,256,1024]{2,1,0:T(8,128)} %fusion.29), kind=kCustom, calls=%fused_computation.2.clone.1 | custom fusion | flops 2097152 | bytes 25165856 | tf_op jit(solution)/shard_map/while/body/eval_jaxpr/scatter-add | solution.py:74
  240.0 5.0 fusion.28
  245.8 6.0 fusion.30
  251.7 17.0 %scatter_fusion.1 = f32[4,256,1024]{2,1,0:T(8,128)} fusion(f32[4,256,1024]{2,1,0:T(8,128)} %get-tuple-element.281, s32[8]{0:T(128)S(1)} %get-tuple-element.264, f32[8,256,1024]{2,1,0:T(8,128)} %fusion.30), kind=kCustom, calls=%fused_computation.3.clone.1 | custom fusion | flops 2097152 | bytes 25165856 | tf_op jit(solution)/shard_map/while/body/eval_jaxpr/scatter-add | solution.py:75
  268.7 7.7 %fusion.29 = f32[8,256,1024]{2,1,0:T(8,128)} fusion(f32[8,256,256]{2,1,0:T(8,128)} %copy-done.8, bf16[8,256,1024]{2,1,0:T(8,128)(2,1)} %gather_fusion.1, pred[8]{0:T(512)(128)(4,1)S(1)} %get-tuple-element.265, f32[8]{0:T(128)S(1)} %compare_convert_fusion.2, bf16[32,256,256]{2,1,0:T(8,128)(2,1)} %get-tuple-element.296, s32[]{:T(128)S(6)} %select_n.90), kind=kOutput, calls=%fused_computation.8.clone.1 | convolution fusion | flops 1077936128 | bytes 15728684 | tf_op jit(solution)/shard_map/while/body/eval_jaxpr/tui,tik->tuk/dot_general | solution.py:68
  276.4 17.3 %scatter_fusion = f32[8,256,1024]{2,1,0:T(8,128)} fusion(f32[8,256,1024]{2,1,0:T(8,128)} %get-tuple-element.280, s32[8]{0:T(128)S(1)} %get-tuple-element.262, f32[8,256,1024]{2,1,0:T(8,128)} %fusion.29), kind=kCustom, calls=%fused_computation.2.clone.1 | custom fusion | flops 2097152 | bytes 25165856 | tf_op jit(solution)/shard_map/while/body/eval_jaxpr/scatter-add | solution.py:74
  301.6 5.0 fusion.28
  307.4 6.0 fusion.30
  313.3 17.3 %scatter_fusion.1 = f32[4,256,1024]{2,1,0:T(8,128)} fusion(f32[4,256,1024]{2,1,0:T(8,128)} %get-tuple-element.281, s32[8]{0:T(128)S(1)} %get-tuple-element.264, f32[8,256,1024]{2,1,0:T(8,128)} %fusion.30), kind=kCustom, calls=%fused_computation.3.clone.1 | custom fusion | flops 2097152 | bytes 25165856 | tf_op jit(solution)/shard_map/while/body/eval_jaxpr/scatter-add | solution.py:75
  330.7 7.7 %fusion.29 = f32[8,256,1024]{2,1,0:T(8,128)} fusion(f32[8,256,256]{2,1,0:T(8,128)} %copy-done.8, bf16[8,256,1024]{2,1,0:T(8,128)(2,1)} %gather_fusion.1, pred[8]{0:T(512)(128)(4,1)S(1)} %get-tuple-element.265, f32[8]{0:T(128)S(1)} %compare_convert_fusion.2, bf16[32,256,256]{2,1,0:T(8,128)(2,1)} %get-tuple-element.296, s32[]{:T(128)S(6)} %select_n.90), kind=kOutput, calls=%fused_computation.8.clone.1 | convolution fusion | flops 1077936128 | bytes 15728684 | tf_op jit(solution)/shard_map/while/body/eval_jaxpr/tui,tik->tuk/dot_general | solution.py:68
  338.4 16.8 %scatter_fusion = f32[8,256,1024]{2,1,0:T(8,128)} fusion(f32[8,256,1024]{2,1,0:T(8,128)} %get-tuple-element.280, s32[8]{0:T(128)S(1)} %get-tuple-element.262, f32[8,256,1024]{2,1,0:T(8,128)} %fusion.29), kind=kCustom, calls=%fused_computation.2.clone.1 | custom fusion | flops 2097152 | bytes 25165856 | tf_op jit(solution)/shard_map/while/body/eval_jaxpr/scatter-add | solution.py:74
  356.3 41.7 %all-reduce = (f32[1024]{0:T(1024)S(1)}, f32[1024]{0:T(1024)S(1)}) all-reduce(f32[1024]{0:T(1024)S(1)} %dynamic_update_slice.6, f32[1024]{0:T(1024)S(1)} %dynamic_update_slice.7), channel_id=1, replica_groups=mesh['user'=8,'item'=4] {'user','item'}, use_global_device_ids=true, to_apply=%region_6.7 | all-reduce | flops 2048 | bytes 16384 | tf_op jit(solution)/shard_map/psum | solution.py:96
  398.1 112.6 %all-reduce.3.cloned.1.call-done = f32[2048,1024]{1,0:T(8,128)} async-done(((f32[2048,1024]{1,0:T(8,128)}), f32[2048,1024]{1,0:T(8,128)}) %all-reduce.3.cloned.1.call-update) | async-done | bytes 8388624 | tf_op jit(solution)/shard_map/psum | solution.py:98
  510.7 6.0 divide_reduce_fusion
  519.8 83.2 %reduce-scatter.2.cloned.1.call-done = f32[1024,128]{1,0:T(8,128)} async-done(((f32[1024,1024]{1,0:T(8,128)}), f32[1024,128]{1,0:T(8,128)}) %reduce-scatter.2.cloned.1.call-update) | async-done | bytes 524304 | tf_op jit(solution)/shard_map/reduce_scatter | solution.py:108
  605.2 20.1 %psum.31 = f32[1024]{0:T(1024)S(1)} all-reduce(f32[1024]{0:T(1024)S(1)} %get-tuple-element.187), channel_id=1, replica_groups=mesh['user'=8,'item'=4] {'user'}, use_global_device_ids=true, to_apply=%region_12.13 | all-reduce | flops 1024 | bytes 8192 | tf_op jit(solution)/shard_map/psum | solution.py:114
  (74 shorter events, 38.2 us)
Async XLA Ops:
  7.2 59.2 %all-gather.5.cloned.1.call-start = ((), (), s32[]{:S(2)}) async-start(), calls=%async_computation.2 | async-start | bytes 2359296 | tf_op jit(solution)/shard_map/all_gather | solution.py:41
  13.2 17.7 %copy-start.7 = (s32[1,1,32]{2,1,0:T(1,128)S(1)}, s32[1,1,32]{2,1,0:T(1,128)}, u32[]{:S(2)}) copy-start(s32[1,1,32]{2,1,0:T(1,128)} %param.17) | copy-start | bytes 388
  13.2 88.5 %all-gather.3.cloned.1.call-start = ((), (), s32[]{:S(2)}) async-start(), calls=%async_computation.1 | async-start | bytes 5242880 | tf_op jit(solution)/shard_map/all_gather | solution.py:40
  30.9 479.8 %all-reduce.3.cloned.1.call-start = ((), (), s32[]{:S(2)}) async-start(), calls=%async_computation.3 | async-start | bytes 16777216 | tf_op jit(solution)/shard_map/psum | solution.py:98
  106.0 2.5 copy-start
  116.4 5.8 copy-start.1
  121.4 6.7 %copy-start.8 = (f32[8,256,256]{2,1,0:T(8,128)}, f32[8,256,256]{2,1,0:T(8,128)S(1)}, u32[]{:S(2)}) copy-start(f32[8,256,256]{2,1,0:T(8,128)S(1)} %fusion.28) | copy-start | bytes 6291460 | tf_op jit(solution)/shard_map/while
  178.1 5.8 copy-start.1
  183.2 6.7 %copy-start.8 = (f32[8,256,256]{2,1,0:T(8,128)}, f32[8,256,256]{2,1,0:T(8,128)S(1)}, u32[]{:S(2)}) copy-start(f32[8,256,256]{2,1,0:T(8,128)S(1)} %fusion.28) | copy-start | bytes 6291460 | tf_op jit(solution)/shard_map/while
  240.0 5.8 copy-start.1
  245.1 6.7 %copy-start.8 = (f32[8,256,256]{2,1,0:T(8,128)}, f32[8,256,256]{2,1,0:T(8,128)S(1)}, u32[]{:S(2)}) copy-start(f32[8,256,256]{2,1,0:T(8,128)S(1)} %fusion.28) | copy-start | bytes 6291460 | tf_op jit(solution)/shard_map/while
  301.6 5.8 copy-start.1
  306.7 6.7 %copy-start.8 = (f32[8,256,256]{2,1,0:T(8,128)}, f32[8,256,256]{2,1,0:T(8,128)S(1)}, u32[]{:S(2)}) copy-start(f32[8,256,256]{2,1,0:T(8,128)S(1)} %fusion.28) | copy-start | bytes 6291460 | tf_op jit(solution)/shard_map/while
  355.2 247.8 %reduce-scatter.2.cloned.1.call-start = ((), (), s32[]{:S(2)}) async-start(), calls=%async_computation.4 | async-start | bytes 4718592 | tf_op jit(solution)/shard_map/reduce_scatter | solution.py:108
  355.2 0.7 copy-start.5
  355.3 0.8 copy-start.6
  355.3 42.8 %copy-start.4 = (f32[1024]{0:T(1024)S(1)}, f32[1024]{0:T(1024)}, u32[]{:S(2)}) copy-start(f32[1024]{0:T(1024)} %param.16) | copy-start | bytes 12292
  355.3 42.8 %copy-start.3 = (f32[2048]{0:T(1024)S(1)}, f32[2048]{0:T(1024)}, u32[]{:S(2)}) copy-start(f32[2048]{0:T(1024)} %param.13) | copy-start | bytes 24580
  517.3 85.7 %copy-start.2 = (bf16[1024,128]{1,0:T(8,128)(2,1)S(1)}, bf16[1024,128]{1,0:T(8,128)(2,1)}, u32[]{:S(2)}) copy-start(bf16[1024,128]{1,0:T(8,128)(2,1)} %get-tuple-element.195) | copy-start | bytes 786436
Sparse Core Ops, SparseCore 0:
  13.3 53.0 all-gather.4
  68.5 33.1 all-gather.2
  355.3 155.3 all-reduce.2
  514.2 88.8 reduce-scatter.1
where the time goes:
time: 633 us; the launch traced here: 632 us
  waiting for transfers between devices  267 us (42%)
  other arithmetic  173 us (27%)
  matrix products  74.9 us (12%)
  blocking collectives  61.8 us (10%)
  local copies, waits for them, and re-layouts  41 us (6%)
  between operations  13.9 us (2%)
    psum x1, waiting for transfers between devices, on_device(): user_summed = lax.psum(user_acc, 'item')  113 us
    reduce_scatter x1, waiting for transfers between devices, on_device(): lax.psum_scatter(item_acc, 'user', scatter_dimension=1, tiled=True)  83.2 us
    scatter-add x4, other arithmetic, group_step(): user_acc = user_acc.at[rows_user].add(user_terms)  69 us
    scatter-add x4, other arithmetic, group_step(): item_acc = item_acc.at[rows_item].add(item_terms)  68.5 us
    psum x1, blocking collectives, on_device(): lax.psum((beta_placed, theta_placed), ('user', 'item'))  41.7 us
    all_gather x1, waiting for transfers between devices, on_device(): beta_full = lax.all_gather(beta_part, 'user', axis=1, tiled=True)  35.5 us
    all_gather x1, waiting for transfers between devices, on_device(): theta_full = lax.all_gather(theta_part, 'item', axis=1, tiled=True)  35.3 us
    dot_general x4, matrix products, group_step(): jnp.einsum('tui,tik->tuk', ratio_tile, items, preferred_element_type=jnp....  30.8 us
  transfers between devices with their start and end apart: 4, of which 4 were waited for; matrix products, arithmetic and copies ran while one was open for 4% of the time, Pallas kernels for 0%

commit v1 on v0

--- a/solution.py
+++ b/solution.py
@@ -38,7 +38,23 @@
     theta_part = exp_mean_log(theta_shape, theta_rate)
     beta_part = exp_mean_log(beta_shape, beta_rate)
     theta_full = lax.all_gather(theta_part, "item", axis=1, tiled=True)
-    beta_full = lax.all_gather(beta_part, "user", axis=1, tiled=True)
+    ways, here, lap = (lax.axis_size("user"), lax.axis_index("user"), beta_part.shape[1])
+    lengths = [n * ways if d == 1 else n for d, n in enumerate(beta_part.shape)]
+    full = lax.dynamic_update_slice_in_dim(
+        jnp.zeros(lengths, beta_part.dtype), beta_part, here * lap, axis=1
+    )
+    going_up = going_down = beta_part
+    for far in range(1, ways // 2 + 1):
+        going_up = lax.ppermute(going_up, "user", [(d, (d + 1) % ways) for d in range(ways)])
+        full = lax.dynamic_update_slice_in_dim(full, going_up, (here - far) % ways * lap, axis=1)
+        if 2 * far < ways:
+            going_down = lax.ppermute(
+                going_down, "user", [(d, (d - 1) % ways) for d in range(ways)]
+            )
+            full = lax.dynamic_update_slice_in_dim(
+                full, going_down, (here + far) % ways * lap, axis=1
+            )
+    beta_full = full
     factors = theta_full.shape[1]
     user_rows = theta_full.shape[0]
     item_rows = beta_full.shape[0]

time: 633 us -> 611 us (0.965)
  waiting for transfers between devices: 267 us -> 227 us
  starting transfers between devices: 0.16 us -> 20.4 us
    all_gather x1 -> x0, waiting for transfers between devices: 35.5 us -> none  [on_device(): beta_full = lax.all_gather(beta_part, 'user', axis=1, tiled=True)]
    all_gather x1, waiting for transfers between devices: 35.3 us -> 0.02 us  [on_device(): theta_full = lax.all_gather(theta_part, 'item', axis=1, tiled=True)]
    ppermute x0 -> x7, waiting for transfers between devices: none -> 30.7 us  [the longest x4 30.7 us: on_device(): lax.ppermute(going_up, 'user', [(d, (d + 1) % ways) for d in range(ways)])]
    ppermute x0 -> x7, starting transfers between devices: none -> 20.3 us  [the longest x4 10.5 us: on_device(): lax.ppermute(going_up, 'user', [(d, (d + 1) % ways) for d in range(ways)])]
    convert_element_type x2 -> x1, other arithmetic: 23.5 us -> 17.6 us  [exp_mean_log(): jnp.exp(lax.digamma(shape_param) - jnp.log(rate_param)).astype(jnp.bfloat16)]
  transfers between devices with their start and end apart: 4 -> 10, of which waited for: 4 -> 6; matrix products, arithmetic and copies ran while one was open for 4% -> 2% of each run, Pallas kernels for 0% -> 0%
where the time goes in v1:
time: 611 us; the launch traced here: 610 us
  waiting for transfers between devices  227 us (37%)
  other arithmetic  171 us (28%)
  matrix products  75.1 us (12%)
  blocking collectives  58.9 us (10%)
  local copies, waits for them, and re-layouts  43.1 us (7%)
  starting transfers between devices  20.4 us (3%)
  between operations  14.1 us (2%)
    psum x1, waiting for transfers between devices, on_device(): user_summed = lax.psum(user_acc, 'item')  113 us
    reduce_scatter x1, waiting for transfers between devices, on_device(): lax.psum_scatter(item_acc, 'user', scatter_dimension=1, tiled=True)  83.4 us
    scatter-add x4, other arithmetic, group_step(): user_acc = user_acc.at[rows_user].add(user_terms)  69 us
    scatter-add x4, other arithmetic, group_step(): item_acc = item_acc.at[rows_item].add(item_terms)  68.1 us
    psum x1, blocking collectives, on_device(): lax.psum((beta_placed, theta_placed), ('user', 'item'))  38.8 us
    dot_general x4, matrix products, group_step(): jnp.einsum('tui,tik->tuk', ratio_tile, items, preferred_element_type=jnp....  30.9 us
    ppermute x4, waiting for transfers between devices, on_device(): lax.ppermute(going_up, 'user', [(d, (d + 1) % ways) for d in range(ways)])  30.7 us
    dot_general x4, matrix products, group_step(): jnp.einsum('tui,tuk->tik', ratio_tile, users, preferred_element_type=jnp....  24 us
  transfers between devices with their start and end apart: 10, of which 6 were waited for; matrix products, arithmetic and copies ran while one was open for 2% of the time, Pallas kernels for 0%

profile of v1, /device:TPU:0, one launch (start us, length us, event | category | flops | bytes accessed | tf_op | source)
XLA Modules:
  0.0 610.1 jit_solution(15432598891383006339)
XLA Ops:
  7.2 17.6 %fusion.16 = (bf16[2048,256]{1,0:T(8,128)(2,1)}, f32[256]{0:T(256)}) fusion(f32[2048,256]{1,0:T(8,128)} %param.12, f32[2048,256]{1,0:T(8,128)} %param.11), kind=kLoop, calls=%fused_computation.36 | loop fusion | flops 41418496 | bytes 5243904 | tf_op jit(solution)/shard_map/convert_element_type | solution.py:20
  36.5 7.5 %collective-permute-done = bf16[1024,128]{1,0:T(8,128)(2,1)S(1)} collective-permute-done((bf16[1024,128]{1,0:T(8,128)(2,1)S(1)}, bf16[1024,128]{1,0:T(8,128)(2,1)S(1)}, u32[]{:S(2)}, u32[]{:S(2)}) %collective-permute-start) | collective-permute-done | bytes 262176 | tf_op jit(solution)/shard_map/ppermute | solution.py:48
  49.7 7.2 %collective-permute-done.2 = bf16[1024,128]{1,0:T(8,128)(2,1)S(1)} collective-permute-done((bf16[1024,128]{1,0:T(8,128)(2,1)S(1)}, bf16[1024,128]{1,0:T(8,128)(2,1)S(1)}, u32[]{:S(2)}, u32[]{:S(2)}) %collective-permute-start.2) | collective-permute-done | bytes 262176 | tf_op jit(solution)/shard_map/ppermute | solution.py:48
  62.8 6.4 %collective-permute-done.4 = bf16[1024,128]{1,0:T(8,128)(2,1)S(1)} collective-permute-done((bf16[1024,128]{1,0:T(8,128)(2,1)S(1)}, bf16[1024,128]{1,0:T(8,128)(2,1)S(1)}, u32[]{:S(2)}, u32[]{:S(2)}) %collective-permute-start.4) | collective-permute-done | bytes 262176 | tf_op jit(solution)/shard_map/ppermute | solution.py:48
  72.0 9.6 %collective-permute-done.6 = bf16[1024,128]{1,0:T(8,128)(2,1)S(1)} collective-permute-done((bf16[1024,128]{1,0:T(8,128)(2,1)S(1)}, bf16[1024,128]{1,0:T(8,128)(2,1)S(1)}, u32[]{:S(2)}, u32[]{:S(2)}) %collective-permute-start.6) | collective-permute-done | bytes 262176 | tf_op jit(solution)/shard_map/ppermute | solution.py:48
  88.4 246.4 %while.15 = (s32[]{:T(128)}, f32[8,256,1024]{2,1,0:T(8,128)}, f32[4,256,1024]{2,1,0:T(8,128)}, s32[32]{0:T(128)S(1)}, bf16[32,256,256]{2,1,0:T(8,128)(2,1)}, /*i...) while((s32[]{:T(128)}, f32[8,256,1024]{2,1,0:T(8,128)}, ...), condition=%wide.region_3.4_spmd, body=%wide.region_0.3_spmd.sunk | while | flops 3238004736 | bytes 134226640 | solution.py:99
  88.5 4.9 gather_fusion
  96.3 5.0 fusion.29
  102.0 6.0 fusion.31
  108.0 16.8 %scatter_fusion.1 = f32[4,256,1024]{2,1,0:T(8,128)} fusion(f32[4,256,1024]{2,1,0:T(8,128)} %get-tuple-element.281, s32[8]{0:T(128)S(1)} %get-tuple-element.264, f32[8,256,1024]{2,1,0:T(8,128)} %fusion.31), kind=kCustom, calls=%fused_computation.3.clone.1 | custom fusion | flops 2097152 | bytes 25165856 | tf_op jit(solution)/shard_map/while/body/eval_jaxpr/scatter-add | solution.py:91
  124.8 7.7 %fusion.30 = f32[8,256,1024]{2,1,0:T(8,128)} fusion(f32[8,256,256]{2,1,0:T(8,128)} %copy-done.11, bf16[8,256,1024]{2,1,0:T(8,128)(2,1)} %gather_fusion.1, pred[8]{0:T(512)(128)(4,1)S(1)} %get-tuple-element.265, f32[8]{0:T(128)S(1)} %compare_convert_fusion.2, bf16[32,256,256]{2,1,0:T(8,128)(2,1)} %get-tuple-element.296, s32[]{:T(128)S(6)} %select_n.156), kind=kOutput, calls=%fused_computation.8.clone.1 | convolution fusion | flops 1077936128 | bytes 15728684 | tf_op jit(solution)/shard_map/while/body/eval_jaxpr/tui,tik->tuk/dot_general | solution.py:84
  132.5 17.4 %scatter_fusion = f32[8,256,1024]{2,1,0:T(8,128)} fusion(f32[8,256,1024]{2,1,0:T(8,128)} %get-tuple-element.280, s32[8]{0:T(128)S(1)} %get-tuple-element.262, f32[8,256,1024]{2,1,0:T(8,128)} %fusion.30), kind=kCustom, calls=%fused_computation.2.clone.1 | custom fusion | flops 2097152 | bytes 25165856 | tf_op jit(solution)/shard_map/while/body/eval_jaxpr/scatter-add | solution.py:90
  157.8 5.0 fusion.29
  163.6 6.0 fusion.31
  169.6 17.1 %scatter_fusion.1 = f32[4,256,1024]{2,1,0:T(8,128)} fusion(f32[4,256,1024]{2,1,0:T(8,128)} %get-tuple-element.281, s32[8]{0:T(128)S(1)} %get-tuple-element.264, f32[8,256,1024]{2,1,0:T(8,128)} %fusion.31), kind=kCustom, calls=%fused_computation.3.clone.1 | custom fusion | flops 2097152 | bytes 25165856 | tf_op jit(solution)/shard_map/while/body/eval_jaxpr/scatter-add | solution.py:91
  186.7 7.7 %fusion.30 = f32[8,256,1024]{2,1,0:T(8,128)} fusion(f32[8,256,256]{2,1,0:T(8,128)} %copy-done.11, bf16[8,256,1024]{2,1,0:T(8,128)(2,1)} %gather_fusion.1, pred[8]{0:T(512)(128)(4,1)S(1)} %get-tuple-element.265, f32[8]{0:T(128)S(1)} %compare_convert_fusion.2, bf16[32,256,256]{2,1,0:T(8,128)(2,1)} %get-tuple-element.296, s32[]{:T(128)S(6)} %select_n.156), kind=kOutput, calls=%fused_computation.8.clone.1 | convolution fusion | flops 1077936128 | bytes 15728684 | tf_op jit(solution)/shard_map/while/body/eval_jaxpr/tui,tik->tuk/dot_general | solution.py:84
  194.4 17.5 %scatter_fusion = f32[8,256,1024]{2,1,0:T(8,128)} fusion(f32[8,256,1024]{2,1,0:T(8,128)} %get-tuple-element.280, s32[8]{0:T(128)S(1)} %get-tuple-element.262, f32[8,256,1024]{2,1,0:T(8,128)} %fusion.30), kind=kCustom, calls=%fused_computation.2.clone.1 | custom fusion | flops 2097152 | bytes 25165856 | tf_op jit(solution)/shard_map/while/body/eval_jaxpr/scatter-add | solution.py:90
  219.7 5.0 fusion.29
  225.5 6.0 fusion.31
  231.5 16.9 %scatter_fusion.1 = f32[4,256,1024]{2,1,0:T(8,128)} fusion(f32[4,256,1024]{2,1,0:T(8,128)} %get-tuple-element.281, s32[8]{0:T(128)S(1)} %get-tuple-element.264, f32[8,256,1024]{2,1,0:T(8,128)} %fusion.31), kind=kCustom, calls=%fused_computation.3.clone.1 | custom fusion | flops 2097152 | bytes 25165856 | tf_op jit(solution)/shard_map/while/body/eval_jaxpr/scatter-add | solution.py:91
  248.4 7.7 %fusion.30 = f32[8,256,1024]{2,1,0:T(8,128)} fusion(f32[8,256,256]{2,1,0:T(8,128)} %copy-done.11, bf16[8,256,1024]{2,1,0:T(8,128)(2,1)} %gather_fusion.1, pred[8]{0:T(512)(128)(4,1)S(1)} %get-tuple-element.265, f32[8]{0:T(128)S(1)} %compare_convert_fusion.2, bf16[32,256,256]{2,1,0:T(8,128)(2,1)} %get-tuple-element.296, s32[]{:T(128)S(6)} %select_n.156), kind=kOutput, calls=%fused_computation.8.clone.1 | convolution fusion | flops 1077936128 | bytes 15728684 | tf_op jit(solution)/shard_map/while/body/eval_jaxpr/tui,tik->tuk/dot_general | solution.py:84
  256.1 17.4 %scatter_fusion = f32[8,256,1024]{2,1,0:T(8,128)} fusion(f32[8,256,1024]{2,1,0:T(8,128)} %get-tuple-element.280, s32[8]{0:T(128)S(1)} %get-tuple-element.262, f32[8,256,1024]{2,1,0:T(8,128)} %fusion.30), kind=kCustom, calls=%fused_computation.2.clone.1 | custom fusion | flops 2097152 | bytes 25165856 | tf_op jit(solution)/shard_map/while/body/eval_jaxpr/scatter-add | solution.py:90
  281.4 5.0 fusion.29
  287.1 6.0 fusion.31
  293.1 17.3 %scatter_fusion.1 = f32[4,256,1024]{2,1,0:T(8,128)} fusion(f32[4,256,1024]{2,1,0:T(8,128)} %get-tuple-element.281, s32[8]{0:T(128)S(1)} %get-tuple-element.264, f32[8,256,1024]{2,1,0:T(8,128)} %fusion.31), kind=kCustom, calls=%fused_computation.3.clone.1 | custom fusion | flops 2097152 | bytes 25165856 | tf_op jit(solution)/shard_map/while/body/eval_jaxpr/scatter-add | solution.py:91
  310.4 7.7 %fusion.30 = f32[8,256,1024]{2,1,0:T(8,128)} fusion(f32[8,256,256]{2,1,0:T(8,128)} %copy-done.11, bf16[8,256,1024]{2,1,0:T(8,128)(2,1)} %gather_fusion.1, pred[8]{0:T(512)(128)(4,1)S(1)} %get-tuple-element.265, f32[8]{0:T(128)S(1)} %compare_convert_fusion.2, bf16[32,256,256]{2,1,0:T(8,128)(2,1)} %get-tuple-element.296, s32[]{:T(128)S(6)} %select_n.156), kind=kOutput, calls=%fused_computation.8.clone.1 | convolution fusion | flops 1077936128 | bytes 15728684 | tf_op jit(solution)/shard_map/while/body/eval_jaxpr/tui,tik->tuk/dot_general | solution.py:84
  318.2 16.7 %scatter_fusion = f32[8,256,1024]{2,1,0:T(8,128)} fusion(f32[8,256,1024]{2,1,0:T(8,128)} %get-tuple-element.280, s32[8]{0:T(128)S(1)} %get-tuple-element.262, f32[8,256,1024]{2,1,0:T(8,128)} %fusion.30), kind=kCustom, calls=%fused_computation.2.clone.1 | custom fusion | flops 2097152 | bytes 25165856 | tf_op jit(solution)/shard_map/while/body/eval_jaxpr/scatter-add | solution.py:90
  336.7 38.8 %all-reduce = (f32[1024]{0:T(1024)S(1)}, f32[1024]{0:T(1024)S(1)}) all-reduce(f32[1024]{0:T(1024)S(1)} %dynamic_update_slice.38, f32[1024]{0:T(1024)S(1)} %dynamic_update_slice.39), channel_id=1, replica_groups=mesh['user'=8,'item'=4] {'user','item'}, use_global_device_ids=true, to_apply=%region_6.7 | all-reduce | flops 2048 | bytes 16384 | tf_op jit(solution)/shard_map/psum | solution.py:112
  375.7 112.6 %all-reduce.3.cloned.1.call-done = f32[2048,1024]{1,0:T(8,128)} async-done(((f32[2048,1024]{1,0:T(8,128)}), f32[2048,1024]{1,0:T(8,128)}) %all-reduce.3.cloned.1.call-update) | async-done | bytes 8388624 | tf_op jit(solution)/shard_map/psum | solution.py:114
  488.3 6.0 divide_reduce_fusion
  497.4 83.4 %reduce-scatter.2.cloned.1.call-done = f32[1024,128]{1,0:T(8,128)} async-done(((f32[1024,1024]{1,0:T(8,128)}), f32[1024,128]{1,0:T(8,128)}) %reduce-scatter.2.cloned.1.call-update) | async-done | bytes 524304 | tf_op jit(solution)/shard_map/reduce_scatter | solution.py:124
  582.9 20.1 %psum.31 = f32[1024]{0:T(1024)S(1)} all-reduce(f32[1024]{0:T(1024)S(1)} %get-tuple-element.187), channel_id=1, replica_groups=mesh['user'=8,'item'=4] {'user'}, use_global_device_ids=true, to_apply=%region_12.13 | all-reduce | flops 1024 | bytes 8192 | tf_op jit(solution)/shard_map/psum | solution.py:130
  (100 shorter events, 69.7 us)
Async XLA Ops:
  7.2 74.5 %all-gather.2.cloned.1.call-start = ((), (), s32[]{:S(2)}) async-start(), calls=%async_computation.1 | async-start | bytes 5242880 | tf_op jit(solution)/shard_map/all_gather | solution.py:40
  24.8 1.0 copy-start.1
  24.8 1.2 copy-start.3
  24.8 24.7 %copy-start.10 = (s32[1,1,32]{2,1,0:T(1,128)S(1)}, s32[1,1,32]{2,1,0:T(1,128)}, u32[]{:S(2)}) copy-start(s32[1,1,32]{2,1,0:T(1,128)} %param.17) | copy-start | bytes 388
  24.8 463.4 %all-reduce.3.cloned.1.call-start = ((), (), s32[]{:S(2)}) async-start(), calls=%async_computation.2 | async-start | bytes 16777216 | tf_op jit(solution)/shard_map/psum | solution.py:114
  29.8 3.1 copy-start.5
  29.8 14.2 %collective-permute-start = (bf16[1024,128]{1,0:T(8,128)(2,1)S(1)}, bf16[1024,128]{1,0:T(8,128)(2,1)S(1)}, u32[]{:S(2)}, u32[]{:S(2)}) collective-permute-start(bf16[1024,128]{1,0:T(8,128)(2,1)S(1)} %get-tuple-element.192), channel_id=1, source_target_pairs={{0,4},{4,8},{8,12},{12,16},{16,20},{20,24},{24,28},{28,0},{1,5},{5... | collective-permute-start | bytes 786440 | tf_op jit(solution)/shard_map/ppermute | solution.py:48
  32.9 13.7 %collective-permute-start.1 = (bf16[1024,128]{1,0:T(8,128)(2,1)S(1)}, bf16[1024,128]{1,0:T(8,128)(2,1)S(1)}, u32[]{:S(2)}, u32[]{:S(2)}) collective-permute-start(bf16[1024,128]{1,0:T(8,128)(2,1)S(1)} %get-tuple-element.192), channel_id=1, source_target_pairs={{0,28},{4,0},{8,4},{12,8},{16,12},{20,16},{24,20},{28,24},{1,29},{... | collective-permute-start | bytes 786440 | tf_op jit(solution)/shard_map/ppermute | solution.py:51
  44.0 12.9 %collective-permute-start.2 = (bf16[1024,128]{1,0:T(8,128)(2,1)S(1)}, bf16[1024,128]{1,0:T(8,128)(2,1)S(1)}, u32[]{:S(2)}, u32[]{:S(2)}) collective-permute-start(bf16[1024,128]{1,0:T(8,128)(2,1)S(1)} %collective-permute-done), channel_id=1, source_target_pairs={{0,4},{4,8},{8,12},{12,16},{16,20},{20,24},{24,28},{28,0},{1,5},{5... | collective-permute-start | bytes 786440 | tf_op jit(solution)/shard_map/ppermute | solution.py:48
  46.5 13.1 %collective-permute-start.3 = (bf16[1024,128]{1,0:T(8,128)(2,1)S(1)}, bf16[1024,128]{1,0:T(8,128)(2,1)S(1)}, u32[]{:S(2)}, u32[]{:S(2)}) collective-permute-start(bf16[1024,128]{1,0:T(8,128)(2,1)S(1)} %collective-permute-done.1), channel_id=1, source_target_pairs={{0,28},{4,0},{8,4},{12,8},{16,12},{20,16},{24,20},{28,24},{1,29},{... | collective-permute-start | bytes 786440 | tf_op jit(solution)/shard_map/ppermute | solution.py:51
  56.9 12.2 %collective-permute-start.4 = (bf16[1024,128]{1,0:T(8,128)(2,1)S(1)}, bf16[1024,128]{1,0:T(8,128)(2,1)S(1)}, u32[]{:S(2)}, u32[]{:S(2)}) collective-permute-start(bf16[1024,128]{1,0:T(8,128)(2,1)S(1)} %collective-permute-done.2), channel_id=1, source_target_pairs={{0,4},{4,8},{8,12},{12,16},{16,20},{20,24},{24,28},{28,0},{1,5},{5... | collective-permute-start | bytes 786440 | tf_op jit(solution)/shard_map/ppermute | solution.py:48
  59.6 12.2 %collective-permute-start.5 = (bf16[1024,128]{1,0:T(8,128)(2,1)S(1)}, bf16[1024,128]{1,0:T(8,128)(2,1)S(1)}, u32[]{:S(2)}, u32[]{:S(2)}) collective-permute-start(bf16[1024,128]{1,0:T(8,128)(2,1)S(1)} %collective-permute-done.3), channel_id=1, source_target_pairs={{0,28},{4,0},{8,4},{12,8},{16,12},{20,16},{24,20},{28,24},{1,29},{... | collective-permute-start | bytes 786440 | tf_op jit(solution)/shard_map/ppermute | solution.py:51
  69.2 12.4 %collective-permute-start.6 = (bf16[1024,128]{1,0:T(8,128)(2,1)S(1)}, bf16[1024,128]{1,0:T(8,128)(2,1)S(1)}, u32[]{:S(2)}, u32[]{:S(2)}) collective-permute-start(bf16[1024,128]{1,0:T(8,128)(2,1)S(1)} %collective-permute-done.4), channel_id=1, source_target_pairs={{0,4},{4,8},{8,12},{12,16},{16,20},{20,24},{24,28},{28,0},{1,5},{5... | collective-permute-start | bytes 786440 | tf_op jit(solution)/shard_map/ppermute | solution.py:48
  96.3 5.8 copy-start
  101.3 6.7 %copy-start.11 = (f32[8,256,256]{2,1,0:T(8,128)}, f32[8,256,256]{2,1,0:T(8,128)S(1)}, u32[]{:S(2)}) copy-start(f32[8,256,256]{2,1,0:T(8,128)S(1)} %fusion.29) | copy-start | bytes 6291460 | tf_op jit(solution)/shard_map/while
  157.8 5.7 copy-start
  162.9 6.7 %copy-start.11 = (f32[8,256,256]{2,1,0:T(8,128)}, f32[8,256,256]{2,1,0:T(8,128)S(1)}, u32[]{:S(2)}) copy-start(f32[8,256,256]{2,1,0:T(8,128)S(1)} %fusion.29) | copy-start | bytes 6291460 | tf_op jit(solution)/shard_map/while
  219.7 5.8 copy-start
  224.8 6.7 %copy-start.11 = (f32[8,256,256]{2,1,0:T(8,128)}, f32[8,256,256]{2,1,0:T(8,128)S(1)}, u32[]{:S(2)}) copy-start(f32[8,256,256]{2,1,0:T(8,128)S(1)} %fusion.29) | copy-start | bytes 6291460 | tf_op jit(solution)/shard_map/while
  281.4 5.8 copy-start
  286.4 6.7 %copy-start.11 = (f32[8,256,256]{2,1,0:T(8,128)}, f32[8,256,256]{2,1,0:T(8,128)S(1)}, u32[]{:S(2)}) copy-start(f32[8,256,256]{2,1,0:T(8,128)S(1)} %fusion.29) | copy-start | bytes 6291460 | tf_op jit(solution)/shard_map/while
  334.9 245.9 %reduce-scatter.2.cloned.1.call-start = ((), (), s32[]{:S(2)}) async-start(), calls=%async_computation.3 | async-start | bytes 4718592 | tf_op jit(solution)/shard_map/reduce_scatter | solution.py:124
  334.9 1.0 copy-start.2
  334.9 1.2 copy-start.4
  334.9 1.6 copy-start.9
  334.9 40.7 %copy-start.8 = (f32[1024]{0:T(1024)S(1)}, f32[1024]{0:T(1024)}, u32[]{:S(2)}) copy-start(f32[1024]{0:T(1024)} %param.16) | copy-start | bytes 12292
  335.0 40.7 %copy-start.7 = (f32[2048]{0:T(1024)S(1)}, f32[2048]{0:T(1024)}, u32[]{:S(2)}) copy-start(f32[2048]{0:T(1024)} %param.13) | copy-start | bytes 24580
  494.9 85.9 %copy-start.6 = (bf16[1024,128]{1,0:T(8,128)(2,1)S(1)}, bf16[1024,128]{1,0:T(8,128)(2,1)}, u32[]{:S(2)}) copy-start(bf16[1024,128]{1,0:T(8,128)(2,1)} %copy-done.5) | copy-start | bytes 786436
Sparse Core Ops, SparseCore 0:
  24.9 37.7 all-gather.1
  335.0 153.2 all-reduce.2
  491.9 88.8 reduce-scatter.1
